TPU v7x, 32 devices: a whole 2x2x4 slice. The times are simulated.
32 devices in a mesh: row: 4 (over y, x), col: 8 (over z, core).
Axes of the slice: x: 2, y: 2, z: 4, core: 2. Of those that a mesh axis runs over, the one named last changes fastest.
Arguments:
- density: float32 [2048, 2048], P('row', 'col'), as said below
- pattern: int32 [16, 16], replicated, may hold values from 0 to 1, as said below
Outputs:
- purified: float32 [2048, 2048], P('row', 'col')
Inputs may be any that keep to these rules, and one draw needn't show every extreme that they name: density is symmetric and zero outside the blocks that pattern allows. pattern is symmetric with ones on its diagonal, and every block row holds exactly 7 ones.
All inputs are finite; a program needn't handle non-finite values.
Results may differ from a plain program's by a relative error of at most 0.0061.
Values may be sent and summed in bfloat16 or wider, within the bound.
No kernel may reach another device: no remote copies, remote signals or barrier semaphores. Data moves between devices by JAX's collectives and lax.ppermute only.
A program may use at most 64 MiB of HBM per device.

v0:
```python
import jax
import jax.numpy as jnp
from jax import lax
from jax.sharding import PartitionSpec as P

BS = 128
STEPS = 2


def allowed_blocks(pattern):
    count = pattern.shape[0]
    index = lax.iota(jnp.int32, count)
    eye = (index[:, None] == index[None, :]).astype(jnp.int32)
    return jnp.maximum(jnp.maximum(pattern, pattern.T), eye)


def apply_mask(values, blocks):
    row_blocks, col_blocks = blocks.shape
    shaped = values.reshape(row_blocks, BS, col_blocks, BS) * blocks[:, None, :, None]
    return shaped.reshape(row_blocks * BS, col_blocks * BS)


def on_device(density, pattern):
    rows, cols = density.shape
    row_blocks = rows // BS
    col_blocks = cols // BS
    allowed = allowed_blocks(pattern)
    first_row = lax.axis_index("row") * row_blocks
    first_col = lax.axis_index("col") * col_blocks
    blocks = lax.dynamic_slice(allowed, (first_row, first_col), (row_blocks, col_blocks)).astype(
        jnp.float32
    )
    current = apply_mask(density, blocks)
    for step in range(STEPS):
        xb = current.astype(jnp.bfloat16)
        x_panel = lax.all_gather(xb, "row", axis=0, tiled=True)
        square = jnp.dot(
            lax.all_gather(xb, "col", axis=1, tiled=True),
            x_panel,
            preferred_element_type=jnp.float32,
        )
        square = apply_mask(square, blocks)
        qb = square.astype(jnp.bfloat16)
        q_panel = lax.all_gather(qb, "row", axis=0, tiled=True)
        total = jnp.dot(
            lax.all_gather(qb, "col", axis=1, tiled=True),
            x_panel,
            preferred_element_type=jnp.float32,
        )
        jordan = total + jnp.dot(
            lax.all_gather(xb, "col", axis=1, tiled=True),
            q_panel,
            preferred_element_type=jnp.float32,
        )
        current = apply_mask(3.0 * square - jordan, blocks)
    return current


def solution(mesh):
    placed = (P("row", "col"), P())
    return jax.shard_map(
        on_device, mesh=mesh, in_specs=placed, out_specs=P("row", "col"), check_vma=False
    )
```

profile of v0, /device:TPU:0, one launch (start us, length us, event | category | flops | bytes accessed | tf_op | source)
XLA Modules:
  0.0 265.3 jit_solution(4661226299853887989)
XLA Ops:
  6.5 0.0 all-gather.11.cloned.1.call-start
  6.5 0.8 copy.3
  7.3 0.8 fusion.7
  8.1 0.2 mul.53
  8.3 1.8 fusion.5
  10.1 0.0 all-gather.11.cloned.1.call-update
  10.1 0.0 all-gather.9.cloned.1.call-start
  10.2 0.7 all-gather.9.cloned.1.call-update
  10.9 0.0 all-gather.13.cloned.1.call-start
  10.9 28.7 %all-gather.11.cloned.1.call-done = bf16[2048,256]{1,0:T(8,128)(2,1)} async-done(((bf16[512,256]{1,0:T(8,128)(2,1)}), bf16[2048,256]{1,0:T(8,128)(2,1)}) %all-gather.11.cloned.1.call-update) | async-done | bytes 1048592 | tf_op jit(solution)/shard_map/all_gather | solution.py:36
  39.6 32.5 %all-gather.9.cloned.1.call-done = bf16[512,2048]{1,0:T(8,128)(2,1)} async-done(((bf16[512,256]{1,0:T(8,128)(2,1)}), bf16[512,2048]{1,0:T(8,128)(2,1)}) %all-gather.9.cloned.1.call-update) | async-done | bytes 2097168 | tf_op jit(solution)/shard_map/all_gather | solution.py:38
  72.0 3.3 %fusion.8 = (bf16[512,256]{1,0:T(8,128)(2,1)}, f32[512,256]{1,0:T(8,128)S(1)}) fusion(f32[64,8,2,128]{3,2,1,0:T(2,128)S(1)} %bitcast.24, bf16[512,2048]{1,0:T(8,128)(2,1)} %all-gather.9.cloned.1.call-done, bf16[2048,256]{1,0:T(8,128)(2,1)} %all-gather.11.cloned.1.call-done), kind=kOutput, calls=%fused_computation.15 | convolution fusion | flops 537133056 | bytes 4456448 | tf_op jit(solution)/shard_map/dot_general | solution.py:37
  75.3 0.0 all-gather.13.cloned.1.call-update
  75.3 0.0 copy-start.1
  75.3 0.0 all-gather.15.cloned.1.call-start
  75.4 0.5 all-gather.15.cloned.1.call-update
  75.9 0.0 all-gather.19.cloned.1.call-start
  76.0 29.4 %all-gather.13.cloned.1.call-done = bf16[512,2048]{1,0:T(8,128)(2,1)} async-done(((bf16[512,256]{1,0:T(8,128)(2,1)}), bf16[512,2048]{1,0:T(8,128)(2,1)}) %all-gather.13.cloned.1.call-update) | async-done | bytes 2097168 | tf_op jit(solution)/shard_map/all_gather | solution.py:46
  105.4 3.4 %fusion.10 = f32[512,256]{1,0:T(8,128)} fusion(bf16[512,2048]{1,0:T(8,128)(2,1)} %all-gather.13.cloned.1.call-done, bf16[2048,256]{1,0:T(8,128)(2,1)} %all-gather.11.cloned.1.call-done), kind=kOutput, calls=%fused_computation.17 | convolution fusion | flops 536870912 | bytes 3670016 | tf_op jit(solution)/shard_map/dot_general | solution.py:45
  108.8 24.1 %all-gather.15.cloned.1.call-done = bf16[2048,256]{1,0:T(8,128)(2,1)} async-done(((bf16[512,256]{1,0:T(8,128)(2,1)}), bf16[2048,256]{1,0:T(8,128)(2,1)}) %all-gather.15.cloned.1.call-update) | async-done | bytes 1048592 | tf_op jit(solution)/shard_map/all_gather | solution.py:44
  132.8 0.0 copy-done.1
  132.8 2.8 %fusion.4 = bf16[512,256]{1,0:T(8,128)(2,1)} fusion(f32[512,256]{1,0:T(8,128)} %fusion.10, bf16[512,2048]{1,0:T(8,128)(2,1)S(1)} %copy-done.1, bf16[2048,256]{1,0:T(8,128)(2,1)} %all-gather.15.cloned.1.call-done, f32[512,256]{1,0:T(8,128)S(1)} %get-tuple-element.6, f32[64,8,2,128]{3,2,1,0:T(2,128)S(1)} %bitcast.25), kind=kOutput, calls=%fused_computation.8 | convolution fusion | flops 537526272 | bytes 4980736 | tf_op jit(solution)/shard_map/dot_general | solution.py:50
  135.6 0.0 all-gather.19.cloned.1.call-update
  135.6 0.0 all-gather.17.cloned.1.call-start
  135.7 0.5 all-gather.17.cloned.1.call-update
  136.2 0.0 all-gather.21.cloned.1.call-start
  136.2 26.1 %all-gather.19.cloned.1.call-done = bf16[2048,256]{1,0:T(8,128)(2,1)} async-done(((bf16[512,256]{1,0:T(8,128)(2,1)}), bf16[2048,256]{1,0:T(8,128)(2,1)}) %all-gather.19.cloned.1.call-update) | async-done | bytes 1048592 | tf_op jit(solution)/shard_map/all_gather | solution.py:36
  162.4 32.3 %all-gather.17.cloned.1.call-done = bf16[512,2048]{1,0:T(8,128)(2,1)} async-done(((bf16[512,256]{1,0:T(8,128)(2,1)}), bf16[512,2048]{1,0:T(8,128)(2,1)}) %all-gather.17.cloned.1.call-update) | async-done | bytes 2097168 | tf_op jit(solution)/shard_map/all_gather | solution.py:38
  194.7 3.3 %fusion.9 = (bf16[512,256]{1,0:T(8,128)(2,1)}, f32[512,256]{1,0:T(8,128)S(1)}) fusion(f32[64,8,2,128]{3,2,1,0:T(2,128)S(1)} %bitcast.26, bf16[512,2048]{1,0:T(8,128)(2,1)} %all-gather.17.cloned.1.call-done, bf16[2048,256]{1,0:T(8,128)(2,1)} %all-gather.19.cloned.1.call-done), kind=kOutput, calls=%fused_computation.16 | convolution fusion | flops 537133056 | bytes 4456448 | tf_op jit(solution)/shard_map/dot_general | solution.py:37
  198.0 0.0 all-gather.21.cloned.1.call-update
  198.0 0.0 copy-start
  198.0 0.0 all-gather.23.cloned.1.call-start
  198.1 0.7 all-gather.23.cloned.1.call-update
  198.8 29.3 %all-gather.21.cloned.1.call-done = bf16[512,2048]{1,0:T(8,128)(2,1)} async-done(((bf16[512,256]{1,0:T(8,128)(2,1)}), bf16[512,2048]{1,0:T(8,128)(2,1)}) %all-gather.21.cloned.1.call-update) | async-done | bytes 2097168 | tf_op jit(solution)/shard_map/all_gather | solution.py:46
  228.1 3.4 %fusion.11 = f32[512,256]{1,0:T(8,128)} fusion(bf16[512,2048]{1,0:T(8,128)(2,1)} %all-gather.21.cloned.1.call-done, bf16[2048,256]{1,0:T(8,128)(2,1)} %all-gather.19.cloned.1.call-done), kind=kOutput, calls=%fused_computation.18 | convolution fusion | flops 536870912 | bytes 3670016 | tf_op jit(solution)/shard_map/dot_general | solution.py:45
  231.4 24.2 %all-gather.23.cloned.1.call-done = bf16[2048,256]{1,0:T(8,128)(2,1)} async-done(((bf16[512,256]{1,0:T(8,128)(2,1)}), bf16[2048,256]{1,0:T(8,128)(2,1)}) %all-gather.23.cloned.1.call-update) | async-done | bytes 1048592 | tf_op jit(solution)/shard_map/all_gather | solution.py:44
  255.6 0.0 copy-done
  255.6 2.9 %fusion.3 = f32[512,256]{1,0:T(8,128)} fusion(f32[512,256]{1,0:T(8,128)} %fusion.11, bf16[512,2048]{1,0:T(8,128)(2,1)S(1)} %copy-done, bf16[2048,256]{1,0:T(8,128)(2,1)} %all-gather.23.cloned.1.call-done, f32[512,256]{1,0:T(8,128)S(1)} %get-tuple-element.8, f32[64,8,2,128]{3,2,1,0:T(2,128)S(1)} %bitcast.27), kind=kOutput, calls=%fused_computation.7 | convolution fusion | flops 537395200 | bytes 5242880 | tf_op jit(solution)/shard_map/dot_general | solution.py:50
Async XLA Ops:
  6.5 33.0 %all-gather.11.cloned.1.call-start = ((), (), s32[]{:S(2)}) async-start(), calls=%async_computation.1 | async-start | bytes 1310720 | tf_op jit(solution)/shard_map/all_gather | solution.py:36
  10.1 61.9 %all-gather.9.cloned.1.call-start = ((), (), s32[]{:S(2)}) async-start(), calls=%async_computation | async-start | bytes 2359296 | tf_op jit(solution)/shard_map/all_gather | solution.py:38
  10.9 94.5 %all-gather.13.cloned.1.call-start = ((), (), s32[]{:S(2)}) async-start(), calls=%async_computation.2 | async-start | bytes 2359296 | tf_op jit(solution)/shard_map/all_gather | solution.py:46
  75.3 57.5 %copy-start.1 = (bf16[512,2048]{1,0:T(8,128)(2,1)S(1)}, bf16[512,2048]{1,0:T(8,128)(2,1)}, u32[]{:S(2)}) copy-start(bf16[512,2048]{1,0:T(8,128)(2,1)} %all-gather.9.cloned.1.call-done) | copy-start | bytes 6291460
  75.3 57.5 %all-gather.15.cloned.1.call-start = ((), (), s32[]{:S(2)}) async-start(), calls=%async_computation.3 | async-start | bytes 1310720 | tf_op jit(solution)/shard_map/all_gather | solution.py:44
  75.9 86.5 %all-gather.19.cloned.1.call-start = ((), (), s32[]{:S(2)}) async-start(), calls=%async_computation.5 | async-start | bytes 1310720 | tf_op jit(solution)/shard_map/all_gather | solution.py:36
  135.6 59.1 %all-gather.17.cloned.1.call-start = ((), (), s32[]{:S(2)}) async-start(), calls=%async_computation.4 | async-start | bytes 2359296 | tf_op jit(solution)/shard_map/all_gather | solution.py:38
  136.2 91.9 %all-gather.21.cloned.1.call-start = ((), (), s32[]{:S(2)}) async-start(), calls=%async_computation.6 | async-start | bytes 2359296 | tf_op jit(solution)/shard_map/all_gather | solution.py:46
  198.0 57.6 %copy-start = (bf16[512,2048]{1,0:T(8,128)(2,1)S(1)}, bf16[512,2048]{1,0:T(8,128)(2,1)}, u32[]{:S(2)}) copy-start(bf16[512,2048]{1,0:T(8,128)(2,1)} %all-gather.17.cloned.1.call-done) | copy-start | bytes 6291460
  198.0 57.6 %all-gather.23.cloned.1.call-start = ((), (), s32[]{:S(2)}) async-start(), calls=%async_computation.7 | async-start | bytes 1310720 | tf_op jit(solution)/shard_map/all_gather | solution.py:44
Sparse Core Ops, SparseCore 0:
  10.2 29.3 all-gather.10
  41.2 30.8 all-gather.8
  75.5 29.8 all-gather.12
  107.1 25.6 all-gather.14
  135.7 26.6 all-gather.18
  163.8 30.8 all-gather.16
  198.1 29.8 all-gather.20
  229.9 25.6 all-gather.22
where the time goes:
time: 266 us; the launch traced here: 265 us
  waiting for transfers between devices  229 us (86%)
  matrix products  18.9 us (7%)
  between operations  13.5 us (5%)
    all_gather x2, waiting for transfers between devices, on_device(): lax.all_gather(xb, 'col', axis=1, tiled=True)  64.8 us
    all_gather x2, waiting for transfers between devices, on_device(): lax.all_gather(qb, 'col', axis=1, tiled=True)  58.7 us
    all_gather x2, waiting for transfers between devices, on_device(): x_panel = lax.all_gather(xb, 'row', axis=0, tiled=True)  54.8 us
    all_gather x2, waiting for transfers between devices, on_device(): q_panel = lax.all_gather(qb, 'row', axis=0, tiled=True)  48.3 us
    dot_general x2, matrix products, on_device(): jnp.dot(lax.all_gather(qb, 'col', axis=1, tiled=True), x_panel, preferred...  6.72 us
    dot_general x2, matrix products, on_device(): jnp.dot(lax.all_gather(xb, 'col', axis=1, tiled=True), x_panel, preferred...  6.54 us
    dot_general x2, matrix products, on_device(): jnp.dot(lax.all_gather(xb, 'col', axis=1, tiled=True), q_panel, preferred...  5.63 us
  transfers between devices with their start and end apart: 8, of which 8 were waited for; matrix products, arithmetic and copies ran while one was open for 3% of the time, Pallas kernels for 0%

commit v1 on v0

--- a/solution.py
+++ b/solution.py
@@ -5,6 +5,17 @@
 
 BS = 128
 STEPS = 2
+
+
+def around_the_ring(shard, axis, dim):
+    devices = lax.axis_size(axis)
+    forward = [(i, (i + 1) % devices) for i in range(devices)]
+    parts = [shard]
+    for far in range(1, devices):
+        parts = [lax.ppermute(parts[0], axis, forward), *parts]
+    out = jnp.concatenate(parts, axis=dim)
+    offset = (lax.axis_index(axis) + 1) * parts[-1].shape[dim]
+    return jnp.roll(out, offset, axis=dim)
 
 
 def allowed_blocks(pattern):
@@ -41,7 +52,7 @@
         )
         square = apply_mask(square, blocks)
         qb = square.astype(jnp.bfloat16)
-        q_panel = lax.all_gather(qb, "row", axis=0, tiled=True)
+        q_panel = around_the_ring(qb, "row", 0)
         total = jnp.dot(
             lax.all_gather(qb, "col", axis=1, tiled=True),
             x_panel,

time: 266 us -> 222 us (0.83)
  waiting for transfers between devices: 229 us -> 176 us
  matrix products: 18.9 us -> 23.3 us
  starting transfers between devices: 0.28 us -> 3.32 us
    all_gather x2 -> x0, waiting for transfers between devices: 48.3 us -> none  [on_device(): q_panel = lax.all_gather(qb, 'row', axis=0, tiled=True)]
    all_gather x2, waiting for transfers between devices: 58.7 us -> 22.5 us  [on_device(): lax.all_gather(qb, 'col', axis=1, tiled=True)]
    ppermute x0 -> x6, waiting for transfers between devices: none -> 33.7 us  [around_the_ring(): parts = [lax.ppermute(parts[0], axis, forward), *parts]]
    dot_general x2, matrix products: 5.63 us -> 11.6 us  [on_device(): jnp.dot(lax.all_gather(xb, 'col', axis=1, tiled=True), q_panel, preferred...]
    ppermute x0 -> x6, starting transfers between devices: none -> 3.12 us  [around_the_ring(): parts = [lax.ppermute(parts[0], axis, forward), *parts]]
  transfers between devices with their start and end apart: 8 -> 12, of which waited for: 8 -> 10; matrix products, arithmetic and copies ran while one was open for 3% -> 2% of each run, Pallas kernels for 0% -> 0%
where the time goes in v1:
time: 222 us; the launch traced here: 221 us
  waiting for transfers between devices  176 us (79%)
  matrix products  23.3 us (10%)
  between operations  13.6 us (6%)
  starting transfers between devices  3.32 us (1%)
  other arithmetic  2.56 us (1%)
    all_gather x2, waiting for transfers between devices, on_device(): lax.all_gather(xb, 'col', axis=1, tiled=True)  64.8 us
    all_gather x2, waiting for transfers between devices, on_device(): x_panel = lax.all_gather(xb, 'row', axis=0, tiled=True)  53.9 us
    ppermute x6, waiting for transfers between devices, around_the_ring(): parts = [lax.ppermute(parts[0], axis, forward), *parts]  33.7 us
    all_gather x2, waiting for transfers between devices, on_device(): lax.all_gather(qb, 'col', axis=1, tiled=True)  22.5 us
    dot_general x2, matrix products, on_device(): jnp.dot(lax.all_gather(xb, 'col', axis=1, tiled=True), q_panel, preferred...  11.6 us
    dot_general x2, matrix products, on_device(): jnp.dot(lax.all_gather(xb, 'col', axis=1, tiled=True), x_panel, preferred...  6.54 us
    dot_general x2, matrix products, on_device(): jnp.dot(lax.all_gather(qb, 'col', axis=1, tiled=True), x_panel, preferred...  5.17 us
  transfers between devices with their start and end apart: 12, of which 10 were waited for; matrix products, arithmetic and copies ran while one was open for 2% of the time, Pallas kernels for 0%

profile of v1, /device:TPU:0, one launch (start us, length us, event | category | flops | bytes accessed | tf_op | source)
XLA Modules:
  0.0 220.7 jit_solution(3040856567917370889)
XLA Ops:
  6.5 0.0 all-gather.9.cloned.1.call-start
  6.5 0.8 copy.3
  7.3 0.8 fusion.27
  8.1 0.2 mul.57
  8.3 1.8 fusion.23
  10.1 0.0 all-gather.9.cloned.1.call-update
  10.1 0.0 all-gather.7.cloned.1.call-start
  10.2 0.7 all-gather.7.cloned.1.call-update
  10.9 0.0 all-gather.11.cloned.1.call-start
  10.9 28.7 %all-gather.9.cloned.1.call-done = bf16[2048,256]{1,0:T(8,128)(2,1)} async-done(((bf16[512,256]{1,0:T(8,128)(2,1)}), bf16[2048,256]{1,0:T(8,128)(2,1)}) %all-gather.9.cloned.1.call-update) | async-done | bytes 1048592 | tf_op jit(solution)/shard_map/all_gather | solution.py:47
  39.6 32.5 %all-gather.7.cloned.1.call-done = bf16[512,2048]{1,0:T(8,128)(2,1)} async-done(((bf16[512,256]{1,0:T(8,128)(2,1)}), bf16[512,2048]{1,0:T(8,128)(2,1)}) %all-gather.7.cloned.1.call-update) | async-done | bytes 2097168 | tf_op jit(solution)/shard_map/all_gather | solution.py:49
  72.0 3.3 %fusion.30 = (bf16[512,256]{1,0:T(8,128)(2,1)}, f32[512,256]{1,0:T(8,128)S(1)}) fusion(f32[64,8,2,128]{3,2,1,0:T(2,128)S(1)} %bitcast.22, bf16[512,2048]{1,0:T(8,128)(2,1)} %all-gather.7.cloned.1.call-done, bf16[2048,256]{1,0:T(8,128)(2,1)} %all-gather.9.cloned.1.call-done), kind=kOutput, calls=%fused_computation.49 | convolution fusion | flops 537133056 | bytes 4456448 | tf_op jit(solution)/shard_map/dot_general | solution.py:48
  75.3 0.0 copy-start
  75.3 0.0 copy-start.2
  75.3 0.0 all-gather.11.cloned.1.call-update
  75.3 0.0 all-gather.15.cloned.1.call-start
  75.4 1.3 collective-permute-start
  76.6 8.5 %collective-permute-done = bf16[512,256]{1,0:T(8,128)(2,1)} collective-permute-done((bf16[512,256]{1,0:T(8,128)(2,1)}, bf16[512,256]{1,0:T(8,128)(2,1)}, u32[]{:S(2)}, u32[]{:S(2)}) %collective-permute-start) | collective-permute-done | bytes 262176 | tf_op jit(solution)/shard_map/ppermute | solution.py:15
  85.1 0.3 collective-permute-start.1
  85.4 8.6 %collective-permute-done.1 = bf16[512,256]{1,0:T(8,128)(2,1)} collective-permute-done((bf16[512,256]{1,0:T(8,128)(2,1)}, bf16[512,256]{1,0:T(8,128)(2,1)}, u32[]{:S(2)}, u32[]{:S(2)}) %collective-permute-start.1) | collective-permute-done | bytes 262176 | tf_op jit(solution)/shard_map/ppermute | solution.py:15
  94.0 0.0 collective-permute-start.2
  94.0 11.4 %all-gather.11.cloned.1.call-done = bf16[512,2048]{1,0:T(8,128)(2,1)} async-done(((bf16[512,256]{1,0:T(8,128)(2,1)}), bf16[512,2048]{1,0:T(8,128)(2,1)}) %all-gather.11.cloned.1.call-update) | async-done | bytes 2097168 | tf_op jit(solution)/shard_map/all_gather | solution.py:57
  105.4 2.6 %fusion.32 = f32[512,256]{1,0:T(8,128)S(1)} fusion(bf16[512,2048]{1,0:T(8,128)(2,1)} %all-gather.11.cloned.1.call-done, bf16[2048,256]{1,0:T(8,128)(2,1)} %all-gather.9.cloned.1.call-done), kind=kOutput, calls=%fused_computation.51 | convolution fusion | flops 536870912 | bytes 3670016 | tf_op jit(solution)/shard_map/dot_general | solution.py:56
  108.0 0.0 collective-permute-done.2
  108.0 0.0 copy-done
  108.0 0.0 copy-done.2
  108.0 5.0 %fusion.4 = bf16[512,256]{1,0:T(8,128)(2,1)} fusion(f32[512,256]{1,0:T(8,128)S(1)} %fusion.32, bf16[512,2048]{1,0:T(8,128)(2,1)S(1)} %copy-done, s32[]{:T(128)S(6)} %select_n.21, bf16[512,256]{1,0:T(8,128)(2,1)} %collective-permute-done.2, bf16[512,256]{1,0:T(8,128)(2,1)} %collective-permute-done.1, bf16[512,256]{1,0:T(8,128)(2,1)} %collective-permute-done, ...), kind=kOutput, calls=%fused_computation.24 | convolution fusion | flops 545914880 | bytes 4980740 | tf_op jit(solution)/shard_map/dot_general | solution.py:61
  113.0 0.0 all-gather.15.cloned.1.call-update
  113.0 0.0 all-gather.13.cloned.1.call-start
  113.1 0.5 all-gather.13.cloned.1.call-update
  113.6 0.0 all-gather.17.cloned.1.call-start
  113.6 25.2 %all-gather.15.cloned.1.call-done = bf16[2048,256]{1,0:T(8,128)(2,1)} async-done(((bf16[512,256]{1,0:T(8,128)(2,1)}), bf16[2048,256]{1,0:T(8,128)(2,1)}) %all-gather.15.cloned.1.call-update) | async-done | bytes 1048592 | tf_op jit(solution)/shard_map/all_gather | solution.py:47
  138.9 32.3 %all-gather.13.cloned.1.call-done = bf16[512,2048]{1,0:T(8,128)(2,1)} async-done(((bf16[512,256]{1,0:T(8,128)(2,1)}), bf16[512,2048]{1,0:T(8,128)(2,1)}) %all-gather.13.cloned.1.call-update) | async-done | bytes 2097168 | tf_op jit(solution)/shard_map/all_gather | solution.py:49
  171.2 3.3 %fusion.31 = (bf16[512,256]{1,0:T(8,128)(2,1)}, f32[512,256]{1,0:T(8,128)S(1)}) fusion(f32[64,8,2,128]{3,2,1,0:T(2,128)S(1)} %bitcast.24, bf16[512,2048]{1,0:T(8,128)(2,1)} %all-gather.13.cloned.1.call-done, bf16[2048,256]{1,0:T(8,128)(2,1)} %all-gather.15.cloned.1.call-done), kind=kOutput, calls=%fused_computation.50 | convolution fusion | flops 537133056 | bytes 4456448 | tf_op jit(solution)/shard_map/dot_general | solution.py:48
  174.4 0.0 copy-start.1
  174.4 0.0 copy-start.3
  174.4 0.0 all-gather.17.cloned.1.call-update
  174.5 1.3 collective-permute-start.3
  175.7 8.4 %collective-permute-done.3 = bf16[512,256]{1,0:T(8,128)(2,1)S(1)} collective-permute-done((bf16[512,256]{1,0:T(8,128)(2,1)}, bf16[512,256]{1,0:T(8,128)(2,1)S(1)}, u32[]{:S(2)}, u32[]{:S(2)}) %collective-permute-start.3) | collective-permute-done | bytes 262176 | tf_op jit(solution)/shard_map/ppermute | solution.py:15
  184.1 0.0 copy-start.4
  184.1 0.7 copy-done.4
  184.8 0.3 collective-permute-start.4
  185.1 8.3 %collective-permute-done.4 = bf16[512,256]{1,0:T(8,128)(2,1)} collective-permute-done((bf16[512,256]{1,0:T(8,128)(2,1)S(1)}, bf16[512,256]{1,0:T(8,128)(2,1)}, u32[]{:S(2)}, u32[]{:S(2)}) %collective-permute-start.4) | collective-permute-done | bytes 262176 | tf_op jit(solution)/shard_map/ppermute | solution.py:15
  193.4 0.0 collective-permute-start.5
  193.4 11.1 %all-gather.17.cloned.1.call-done = bf16[512,2048]{1,0:T(8,128)(2,1)} async-done(((bf16[512,256]{1,0:T(8,128)(2,1)}), bf16[512,2048]{1,0:T(8,128)(2,1)}) %all-gather.17.cloned.1.call-update) | async-done | bytes 2097168 | tf_op jit(solution)/shard_map/all_gather | solution.py:57
  204.5 0.0 copy-start.5
  204.5 2.6 %fusion.33 = f32[512,256]{1,0:T(8,128)S(1)} fusion(bf16[512,2048]{1,0:T(8,128)(2,1)} %all-gather.17.cloned.1.call-done, bf16[2048,256]{1,0:T(8,128)(2,1)} %all-gather.15.cloned.1.call-done), kind=kOutput, calls=%fused_computation.52 | convolution fusion | flops 536870912 | bytes 3670016 | tf_op jit(solution)/shard_map/dot_general | solution.py:56
  207.1 0.0 collective-permute-done.5
  207.1 0.0 copy-done.1
  207.2 0.0 copy-done.3
  207.2 0.0 copy-done.5
  207.2 6.6 %fusion.3 = f32[512,256]{1,0:T(8,128)} fusion(f32[512,256]{1,0:T(8,128)S(1)} %fusion.33, bf16[512,2048]{1,0:T(8,128)(2,1)S(1)} %copy-done.1, s32[]{:T(128)S(6)} %select_n.21, bf16[512,256]{1,0:T(8,128)(2,1)} %collective-permute-done.5, bf16[512,256]{1,0:T(8,128)(2,1)} %collective-permute-done.4, bf16[512,256]{1,0:T(8,128)(2,1)S(1)} %copy-done.5, ...), kind=kOutput, calls=%fused_computation.23 | convolution fusion | flops 545783808 | bytes 5242884 | tf_op jit(solution)/shard_map/dot_general | solution.py:61
Async XLA Ops:
  6.5 33.0 %all-gather.9.cloned.1.call-start = ((), (), s32[]{:S(2)}) async-start(), calls=%async_computation.1 | async-start | bytes 1310720 | tf_op jit(solution)/shard_map/all_gather | solution.py:47
  10.1 61.9 %all-gather.7.cloned.1.call-start = ((), (), s32[]{:S(2)}) async-start(), calls=%async_computation | async-start | bytes 2359296 | tf_op jit(solution)/shard_map/all_gather | solution.py:49
  10.9 94.5 %all-gather.11.cloned.1.call-start = ((), (), s32[]{:S(2)}) async-start(), calls=%async_computation.2 | async-start | bytes 2359296 | tf_op jit(solution)/shard_map/all_gather | solution.py:57
  75.3 32.7 %copy-start = (bf16[512,2048]{1,0:T(8,128)(2,1)S(1)}, bf16[512,2048]{1,0:T(8,128)(2,1)}, u32[]{:S(2)}) copy-start(bf16[512,2048]{1,0:T(8,128)(2,1)} %all-gather.7.cloned.1.call-done) | copy-start | bytes 6291460
  75.3 32.7 %copy-start.2 = (bf16[512,256]{1,0:T(8,128)(2,1)S(1)}, bf16[512,256]{1,0:T(8,128)(2,1)}, u32[]{:S(2)}) copy-start(bf16[512,256]{1,0:T(8,128)(2,1)} %get-tuple-element.6) | copy-start | bytes 786436
  75.3 63.5 %all-gather.15.cloned.1.call-start = ((), (), s32[]{:S(2)}) async-start(), calls=%async_computation.4 | async-start | bytes 1310720 | tf_op jit(solution)/shard_map/all_gather | solution.py:47
  75.4 9.7 %collective-permute-start = (bf16[512,256]{1,0:T(8,128)(2,1)}, bf16[512,256]{1,0:T(8,128)(2,1)}, u32[]{:S(2)}, u32[]{:S(2)}) collective-permute-start(bf16[512,256]{1,0:T(8,128)(2,1)} %get-tuple-element.6), channel_id=1, source_target_pairs={{0,8},{8,16},{16,24},{24,0},{1,9},{9,17},{17,25},{25,1},{2,10},{10... | collective-permute-start | bytes 786440 | tf_op jit(solution)/shard_map/ppermute | solution.py:15
  85.1 8.9 %collective-permute-start.1 = (bf16[512,256]{1,0:T(8,128)(2,1)}, bf16[512,256]{1,0:T(8,128)(2,1)}, u32[]{:S(2)}, u32[]{:S(2)}) collective-permute-start(bf16[512,256]{1,0:T(8,128)(2,1)} %collective-permute-done), channel_id=1, source_target_pairs={{0,8},{8,16},{16,24},{24,0},{1,9},{9,17},{17,25},{25,1},{2,10},{10... | collective-permute-start | bytes 786440 | tf_op jit(solution)/shard_map/ppermute | solution.py:15
  94.0 14.0 %collective-permute-start.2 = (bf16[512,256]{1,0:T(8,128)(2,1)}, bf16[512,256]{1,0:T(8,128)(2,1)}, u32[]{:S(2)}, u32[]{:S(2)}) collective-permute-start(bf16[512,256]{1,0:T(8,128)(2,1)} %collective-permute-done.1), channel_id=1, source_target_pairs={{0,8},{8,16},{16,24},{24,0},{1,9},{9,17},{17,25},{25,1},{2,10},{10... | collective-permute-start | bytes 786440 | tf_op jit(solution)/shard_map/ppermute | solution.py:15
  113.0 58.2 %all-gather.13.cloned.1.call-start = ((), (), s32[]{:S(2)}) async-start(), calls=%async_computation.3 | async-start | bytes 2359296 | tf_op jit(solution)/shard_map/all_gather | solution.py:49
  113.6 90.9 %all-gather.17.cloned.1.call-start = ((), (), s32[]{:S(2)}) async-start(), calls=%async_computation.5 | async-start | bytes 2359296 | tf_op jit(solution)/shard_map/all_gather | solution.py:57
  174.4 32.7 %copy-start.1 = (bf16[512,2048]{1,0:T(8,128)(2,1)S(1)}, bf16[512,2048]{1,0:T(8,128)(2,1)}, u32[]{:S(2)}) copy-start(bf16[512,2048]{1,0:T(8,128)(2,1)} %all-gather.13.cloned.1.call-done) | copy-start | bytes 6291460
  174.4 32.7 %copy-start.3 = (bf16[512,256]{1,0:T(8,128)(2,1)S(1)}, bf16[512,256]{1,0:T(8,128)(2,1)}, u32[]{:S(2)}) copy-start(bf16[512,256]{1,0:T(8,128)(2,1)} %get-tuple-element.8) | copy-start | bytes 786436
  174.5 9.6 %collective-permute-start.3 = (bf16[512,256]{1,0:T(8,128)(2,1)}, bf16[512,256]{1,0:T(8,128)(2,1)S(1)}, u32[]{:S(2)}, u32[]{:S(2)}) collective-permute-start(bf16[512,256]{1,0:T(8,128)(2,1)} %get-tuple-element.8), channel_id=1, source_target_pairs={{0,8},{8,16},{16,24},{24,0},{1,9},{9,17},{17,25},{25,1},{2,10},{10... | collective-permute-start | bytes 786440 | tf_op jit(solution)/shard_map/ppermute | solution.py:15
  184.1 0.7 copy-start.4
  184.8 8.7 %collective-permute-start.4 = (bf16[512,256]{1,0:T(8,128)(2,1)S(1)}, bf16[512,256]{1,0:T(8,128)(2,1)}, u32[]{:S(2)}, u32[]{:S(2)}) collective-permute-start(bf16[512,256]{1,0:T(8,128)(2,1)S(1)} %collective-permute-done.3), channel_id=1, source_target_pairs={{0,8},{8,16},{16,24},{24,0},{1,9},{9,17},{17,25},{25,1},{2,10},{10... | collective-permute-start | bytes 786440 | tf_op jit(solution)/shard_map/ppermute | solution.py:15
  193.4 13.7 %collective-permute-start.5 = (bf16[512,256]{1,0:T(8,128)(2,1)}, bf16[512,256]{1,0:T(8,128)(2,1)}, u32[]{:S(2)}, u32[]{:S(2)}) collective-permute-start(bf16[512,256]{1,0:T(8,128)(2,1)} %collective-permute-done.4), channel_id=1, source_target_pairs={{0,8},{8,16},{16,24},{24,0},{1,9},{9,17},{17,25},{25,1},{2,10},{10... | collective-permute-start | bytes 786440 | tf_op jit(solution)/shard_map/ppermute | solution.py:15
  204.5 2.6 %copy-start.5 = (bf16[512,256]{1,0:T(8,128)(2,1)S(1)}, bf16[512,256]{1,0:T(8,128)(2,1)}, u32[]{:S(2)}) copy-start(bf16[512,256]{1,0:T(8,128)(2,1)} %copy-done.4) | copy-start | bytes 786436
Sparse Core Ops, SparseCore 0:
  10.2 29.3 all-gather.8
  41.2 30.8 all-gather.6
  75.5 29.8 all-gather.10
  113.1 25.6 all-gather.14
  140.3 30.8 all-gather.12
  174.6 29.8 all-gather.16
